TPU v7x, 32 devices: a whole 2x2x4 slice. The times are simulated.
32 devices in a mesh: ctx: 4 (over y, core), row: 8 (over z, x).
Axes of the slice: x: 2, y: 2, z: 4, core: 2. Of those that a mesh axis runs over, the one named last changes fastest.
Arguments:
- queries: bfloat16 [16, 2, 4096], P('row'), may hold values from -400 to 400
- prefix_id: int32 [16], P('row'), may hold values from 0 to 7
- prefix_keys: bfloat16 [8, 1024, 512], P(None, ('ctx', 'row')), may hold values from -8 to 8
- prefix_values: bfloat16 [8, 1024, 512], P(None, ('ctx', 'row')), may hold values from -6 to 6
- pool_keys: bfloat16 [512, 64, 512], P(('ctx', 'row')), may hold values from -5 to 5
- pool_values: bfloat16 [512, 64, 512], P(('ctx', 'row')), may hold values from -6 to 6
- page_table: int32 [16, 32], P('row'), may hold values from 0 to 511, as said below
- suffix_len: int32 [16], P('row'), may hold values from 256 to 2048
- new_keys: bfloat16 [16, 2, 512], P('row'), may hold values from -6.25 to 6.25
- new_values: bfloat16 [16, 2, 512], P('row'), may hold values from -6 to 6
Outputs:
- attended: bfloat16 [16, 2, 4096], P('row')
Inputs may be any that keep to these rules, and one draw needn't show every extreme that they name: `page_table`: the 64 entries of the rows i with one value of i // 2 name different pool pages p with (p // 16) % (8) == i // 2, and together they name all such pages.
All inputs are finite; a program needn't handle non-finite values.
Results may differ from a plain program's by a relative error of at most 0.003.
Values may be sent and summed in bfloat16 or wider, within the bound.
No kernel may reach another device: no remote copies, remote signals or barrier semaphores. Data moves between devices by JAX's collectives and lax.ppermute only.
A program may use at most 64 MiB of HBM per device.

v0:
```python
import math
import jax
import jax.numpy as jnp
from jax import lax
from jax.sharding import PartitionSpec as P

H = 32
KVH = 4
HD = 128
LANES = 128
MASKED_SCORE = -1e30


def block_stats(scores, valid_mask, values, einsum_form):
    block_peak = jnp.max(jnp.where(valid_mask, scores, MASKED_SCORE), axis=-1)
    weights = jnp.where(valid_mask, jnp.exp(scores - block_peak[..., None]), 0.0).astype(
        jnp.bfloat16
    )
    block_total = jnp.sum(weights.astype(jnp.float32), axis=-1)
    block_sum = jnp.einsum(einsum_form, weights, values, preferred_element_type=jnp.float32)
    return (block_peak, block_total, block_sum)


def combine_pair(earlier, later):
    highest = jnp.maximum(earlier[0], later[0])
    left_factor = jnp.exp(earlier[0] - highest)
    right_factor = jnp.exp(later[0] - highest)
    totals = left_factor * earlier[1] + right_factor * later[1]
    sums = left_factor[..., None] * earlier[2] + right_factor[..., None] * later[2]
    return (highest, totals, sums)


def per_device(
    queries,
    prefix_id,
    prefix_keys,
    prefix_values,
    pool_keys,
    pool_values,
    page_table,
    suffix_len,
    new_keys,
    new_values,
):
    rows_dev, step_count, feature_width = queries.shape
    groups = H // KVH
    score_scale = 1.0 / math.sqrt(HD)
    row_count = lax.axis_size("row")
    ctx_count = lax.axis_size("ctx")
    row_index = lax.axis_index("row")
    ctx_index = lax.axis_index("ctx")
    flat_index = ctx_index * row_count + row_index
    own_query = queries.reshape(rows_dev, step_count, KVH, groups, HD)
    slot_count, page_len, kv_width = pool_keys.shape
    slot_ids = flat_index * slot_count + jnp.arange(slot_count, dtype=jnp.int32)
    slot_match = page_table[:, :, None] == slot_ids[None, None, :]
    entry_pos = jnp.arange(page_table.shape[1], dtype=jnp.int32)
    page_of = jnp.sum(jnp.where(slot_match, entry_pos[None, :, None], 0), axis=1)
    owned = jnp.any(slot_match, axis=1)
    token_pos = (
        page_of[:, :, None] * page_len + jnp.arange(page_len, dtype=jnp.int32)[None, None, :]
    )
    live_mask = owned[:, :, None] & (token_pos < suffix_len[:, None, None])
    live_mask = live_mask.reshape(rows_dev, 1, 1, 1, slot_count * page_len)
    flat_keys = pool_keys.reshape(slot_count * page_len, KVH, HD)
    flat_values = pool_values.reshape(slot_count * page_len, KVH, HD)
    suffix_scores = (
        jnp.einsum("rskgd,tkd->rskgt", own_query, flat_keys, preferred_element_type=jnp.float32)
        * score_scale
    )
    suffix_stats = block_stats(suffix_scores, live_mask, flat_values, "rskgt,tkd->rskgd")
    fresh_keys = new_keys.reshape(rows_dev, step_count, KVH, HD)
    fresh_values = new_values.reshape(rows_dev, step_count, KVH, HD)
    fresh_scores = (
        jnp.einsum("rskgd,rtkd->rskgt", own_query, fresh_keys, preferred_element_type=jnp.float32)
        * score_scale
    )
    causal = jnp.arange(step_count)[None, :] <= jnp.arange(step_count)[:, None]
    causal = causal.reshape(1, step_count, 1, 1, step_count)
    fresh_stats = block_stats(fresh_scores, causal, fresh_values, "rskgt,rtkd->rskgd")
    query_cols = step_count * feature_width
    id_cols = jnp.broadcast_to(prefix_id.astype(jnp.bfloat16)[:, None], (rows_dev, LANES))
    packed = jnp.concatenate([queries.reshape(rows_dev, query_cols), id_cols], axis=1)
    gathered = lax.all_gather(packed, "row", axis=0, tiled=True)
    total_rows = gathered.shape[0]
    every_query = gathered[:, :query_cols].reshape(total_rows, step_count, KVH, groups, HD)
    every_prefix = gathered[:, query_cols].astype(jnp.int32)
    span_len = prefix_keys.shape[1]
    row_keys = jnp.take(prefix_keys, every_prefix, axis=0).reshape(total_rows, span_len, KVH, HD)
    row_values = jnp.take(prefix_values, every_prefix, axis=0).reshape(
        total_rows, span_len, KVH, HD
    )
    prefix_scores = (
        jnp.einsum("rskgd,rtkd->rskgt", every_query, row_keys, preferred_element_type=jnp.float32)
        * score_scale
    )
    always = jnp.ones((1, 1, 1, 1, span_len), dtype=bool)
    prefix_stats = block_stats(prefix_scores, always, row_values, "rskgt,rtkd->rskgd")
    row_start = row_index * rows_dev
    own_prefix = tuple(
        (lax.dynamic_slice_in_dim(member, row_start, rows_dev, 0) for member in prefix_stats)
    )
    own_merged = combine_pair(own_prefix, suffix_stats)
    peak_all, total_all, sum_all = tuple(
        (
            lax.dynamic_update_slice_in_dim(whole_arr, piece_arr, row_start, 0)
            for whole_arr, piece_arr in zip(prefix_stats, own_merged)
        )
    )
    units = rows_dev * step_count * H
    share = units // ctx_count
    pt_rows = -(-2 * share // LANES)
    peak_u = peak_all.reshape(row_count, ctx_count, share)
    total_u = total_all.reshape(row_count, ctx_count, share)
    sum_u = sum_all.reshape(row_count, ctx_count, share, HD)
    pt = jnp.concatenate([peak_u, total_u], axis=-1)
    pt = jnp.pad(pt, ((0, 0), (0, 0), (0, pt_rows * LANES - 2 * share)))
    pt = pt.reshape(row_count, ctx_count, pt_rows, LANES)
    outgoing = jnp.concatenate([sum_u, pt], axis=2)
    outgoing = jnp.swapaxes(outgoing, 0, 1).reshape(ctx_count * row_count, share + pt_rows, LANES)
    incoming = lax.all_to_all(outgoing, ("ctx", "row"), split_axis=0, concat_axis=0, tiled=True)
    sources = incoming.shape[0]
    got_sum = incoming[:, :share, :]
    got_pt = incoming[:, share:, :].reshape(sources, pt_rows * LANES)
    got_peak = got_pt[:, :share]
    got_total = got_pt[:, share : 2 * share]
    unit_start = ctx_index * share
    fresh_peak = lax.dynamic_slice_in_dim(fresh_stats[0].reshape(units), unit_start, share)
    fresh_total = lax.dynamic_slice_in_dim(fresh_stats[1].reshape(units), unit_start, share)
    fresh_sum = lax.dynamic_slice_in_dim(fresh_stats[2].reshape(units, HD), unit_start, share)
    top = jnp.maximum(jnp.max(got_peak, axis=0), fresh_peak)
    factor = jnp.exp(got_peak - top[None])
    fresh_factor = jnp.exp(fresh_peak - top)
    denom = jnp.sum(factor * got_total, axis=0) + fresh_factor * fresh_total
    numer = jnp.sum(factor[..., None] * got_sum, axis=0) + fresh_factor[..., None] * fresh_sum
    result = (numer / denom[..., None]).astype(jnp.bfloat16)
    whole = lax.all_gather(result, "ctx", axis=0, tiled=True)
    return whole.reshape(rows_dev, step_count, H * HD)


def solution(mesh):
    in_specs = (
        P("row", None, None),
        P("row"),
        P(None, ("ctx", "row"), None),
        P(None, ("ctx", "row"), None),
        P(("ctx", "row"), None, None),
        P(("ctx", "row"), None, None),
        P("row", None),
        P("row"),
        P("row", None, None),
        P("row", None, None),
    )
    out_specs = P("row", None, None)
    return jax.shard_map(
        per_device, mesh=mesh, in_specs=in_specs, out_specs=out_specs, check_vma=False
    )
```

profile of v0, /device:TPU:0, one launch (start us, length us, event | category | flops | bytes accessed | tf_op | source)
XLA Modules:
  0.0 77.9 jit_solution(5196668622109800049)
XLA Ops:
  0.0 0.7 convert_element_type.32
  0.7 0.8 %copy.117 = bf16[1,2,2,4096]{3,1,2,0:T(2,128)(2,1)S(1)} copy(bf16[1,2,2,4096]{3,2,1,0:T(2,128)(2,1)} %bitcast.69) | data formatting | bytes 65536
  1.6 32.5 %all-gather = bf16[8,2,8320]{2,1,0:T(2,128)(2,1)S(1)} all-gather(bf16[1,2,8320]{2,1,0:T(2,128)(2,1)S(1)} %maximum_bitcast_fusion.1), channel_id=1, replica_groups=mesh['ctx'=4,'row'=8] {'row'}, dimensions={0}, use_global_device_ids=true | all-gather | bytes 299520 | tf_op jit(solution)/shard_map/all_gather | solution.py:84
  34.2 0.1 reshape.165
  34.3 0.1 convert_reduce_fusion.3
  34.5 0.7 copy-done.10
  35.1 0.2 compare_reduce_fusion
  35.3 0.2 fusion.16
  35.6 0.6 gather_fusion
  36.2 0.4 copy-done.3
  36.5 0.6 gather_fusion.1
  37.1 0.2 broadcast_select_fusion.1
  37.3 0.1 reshape.127
  37.5 0.1 reshape.128
  37.6 0.5 fusion.22
  38.1 0.5 convert_reduce_fusion.1
  38.6 0.3 fusion.10
  39.0 0.1 and.21
  39.2 0.1 add.71
  39.3 0.5 copy-done.1
  39.8 0.3 reshape.130
  40.1 0.6 copy-done.11
  40.7 0.1 compare_and_fusion
  40.8 0.5 select_reduce_fusion
  41.4 0.9 %convert_reduce_fusion = (f32[2,2,4,8]{3,1,0,2:T(2,128)S(1)}, bf16[2,2,4,8,1024]{4,3,1,0,2:T(8,128)(2,1)}) fusion(f32[2,2,4,8,1024]{4,3,1,0,2:T(8,128)S(1)} %get-tuple-element.23, f32[2,2,4,8]{3,1,0,2:T(2,128)S(1)} %get-tuple-element.22, pred[2,1024]{1,0:T(4,128)(4,1)S(1)} %compare_and_fusion), kind=kLoop, calls=%fused_computation.22 | loop fusion | flops 655232 | bytes 789504 | tf_op jit(solution)/shard_map/reduce_sum | solution.py:19
  42.2 0.6 fusion.19
  42.9 0.1 reshape.135
  43.0 0.1 reshape.134
  43.2 0.3 reshape.132
  43.5 0.4 copy-done.7
  43.9 1.2 %fusion.4 = f32[16,2,4,8,128]{4,3,1,2,0:T(8,128)S(1)} fusion(f32[16,2,4,8,128]{4,3,1,2,0:T(8,128)S(1)} %copy.164, s32[]{:T(128)S(6)} %select_n.41, bf16[1024,4,128,1,1]{2,1,0,4,3:T(4,128)(2,1)S(1)} %bitcast.63, bf16[2,2,4,8,1024]{4,3,1,0,2:T(8,128)(2,1)} %get-tuple-element.16, f32[16,4,128,2,8]{2,4,3,1,0:T(8,128)S(1)} %fusion.10, ...), kind=kOutput, calls=%fused_computation.10 | convolution fusion | flops 33603584 | bytes 1458180 | tf_op jit(solution)/shard_map/rskgt,tkd->rskgd/dot_general | solution.py:20
  45.2 0.1 select_maximum_fusion
  45.3 0.3 copy.161
  45.7 1.2 %copy.96 = f32[32,33,128]{2,1,0:T(8,128)} copy(f32[32,33,128]{2,0,1:T(8,128)S(1)} %bitcast.59) | data formatting | bytes 1081344 | tf_op jit(solution)/shard_map/reshape | solution.py:120
  46.8 5.5 %all-to-all-start = ((f32[32,33,128]{2,1,0:T(8,128)}), f32[32,33,128]{2,1,0:T(8,128)S(1)}, u32[]{:S(2)}, u32[]{:S(2)}) async-start(f32[32,33,128]{2,1,0:T(8,128)} %copy.96), calls=%async_computation | async-start | bytes 1310720 | tf_op jit(solution)/shard_map/all_to_all | solution.py:121
  52.4 0.3 select_reduce_fusion.1
  52.7 0.1 reshape.140
  52.8 0.1 convert_reduce_fusion.2
  52.9 0.2 convolution_bitcast_fusion
  53.1 0.1 reshape.143
  53.2 18.3 %all-to-all-done = f32[32,33,128]{2,1,0:T(8,128)S(1)} async-done(((f32[32,33,128]{2,1,0:T(8,128)}), f32[32,33,128]{2,1,0:T(8,128)S(1)}, u32[]{:S(2)}, u32[]{:S(2)}) %all-to-all-start) | async-done | bytes 540704 | tf_op jit(solution)/shard_map/all_to_all | solution.py:121
  71.6 0.1 dynamic-slice_maximum_fusion
  71.6 0.1 fusion.17
  71.7 0.1 multiply_add_fusion
  71.8 0.2 fusion.8
  72.0 0.1 divide_convert_fusion
  72.1 5.2 %all_gather.7 = bf16[128,128]{1,0:T(8,128)(2,1)S(1)} all-gather(bf16[32,128]{1,0:T(8,128)(2,1)S(1)} %divide_convert_fusion), channel_id=1, replica_groups=mesh['ctx'=4,'row'=8] {'ctx'}, dimensions={0}, use_global_device_ids=true | all-gather | bytes 40960 | tf_op jit(solution)/shard_map/all_gather | solution.py:137
  77.3 0.6 reshape.144
  (46 shorter events, 0.8 us)
Async XLA Ops:
  0.0 35.6 %copy-start = (bf16[8,32,512]{2,1,0:T(8,128)(2,1)S(1)}, bf16[8,32,512]{2,1,0:T(8,128)(2,1)}, u32[]{:S(2)}) copy-start(bf16[8,32,512]{2,1,0:T(8,128)(2,1)} %param.15) | copy-start | bytes 786436
  34.4 1.1 %copy-start.4 = (bf16[2,2,4096]{2,1,0:T(2,128)(2,1)S(1)}, bf16[2,2,4096]{2,1,0:T(2,128)(2,1)}, u32[]{:S(2)}) copy-start(bf16[2,2,4096]{2,1,0:T(2,128)(2,1)} %param.12) | copy-start | bytes 98308
  34.4 0.7 copy-start.10
  35.5 5.3 %copy-start.5 = (bf16[2,2,4,8,128]{4,3,2,1,0:T(8,128)(2,1)}, bf16[2,2,4,8,128]{4,3,2,1,0:T(8,128)(2,1)S(1)}, u32[]{:S(2)}) copy-start(bf16[2,2,4,8,128]{4,3,2,1,0:T(8,128)(2,1)S(1)} %reshape.131) | copy-start | bytes 98308
  35.6 1.0 %copy-start.3 = (bf16[8,32,512]{2,1,0:T(8,128)(2,1)S(1)}, bf16[8,32,512]{2,1,0:T(8,128)(2,1)}, u32[]{:S(2)}) copy-start(bf16[8,32,512]{2,1,0:T(8,128)(2,1)} %param.14) | copy-start | bytes 786436
  38.6 1.2 %copy-start.1 = (bf16[16,64,512]{2,1,0:T(8,128)(2,1)S(1)}, bf16[16,64,512]{2,1,0:T(8,128)(2,1)}, u32[]{:S(2)}) copy-start(bf16[16,64,512]{2,1,0:T(8,128)(2,1)} %param.16) | copy-start | bytes 3145732
  40.1 0.7 copy-start.11
  41.4 1.8 %copy-start.2 = (bf16[16,64,512]{2,1,0:T(8,128)(2,1)S(1)}, bf16[16,64,512]{2,1,0:T(8,128)(2,1)}, u32[]{:S(2)}) copy-start(bf16[16,64,512]{2,1,0:T(8,128)(2,1)} %param.17) | copy-start | bytes 3145732
  43.2 0.7 copy-start.7
  43.2 0.7 copy-start.8
  46.8 5.6 %copy-start.6 = (bf16[2,2,4,8,128]{4,3,2,1,0:T(8,128)(2,1)S(1)}, bf16[2,2,4,8,128]{4,3,2,1,0:T(8,128)(2,1)}, u32[]{:S(2)}) copy-start(bf16[2,2,4,8,128]{4,3,2,1,0:T(8,128)(2,1)} %copy-done.5) | copy-start | bytes 98308
  46.8 5.6 %copy-start.12 = (bf16[2,2,512]{2,1,0:T(2,128)(2,1)S(1)}, bf16[2,2,512]{2,1,0:T(2,128)(2,1)}, u32[]{:S(2)}) copy-start(bf16[2,2,512]{2,1,0:T(2,128)(2,1)} %param.20) | copy-start | bytes 12292
  46.8 6.1 %copy-start.9 = (bf16[2,2,512]{2,1,0:T(2,128)(2,1)S(1)}, bf16[2,2,512]{2,1,0:T(2,128)(2,1)}, u32[]{:S(2)}) copy-start(bf16[2,2,512]{2,1,0:T(2,128)(2,1)} %param.21) | copy-start | bytes 12292
  46.8 24.7 %all-to-all-start = ((f32[32,33,128]{2,1,0:T(8,128)}), f32[32,33,128]{2,1,0:T(8,128)S(1)}, u32[]{:S(2)}, u32[]{:S(2)}) async-start(f32[32,33,128]{2,1,0:T(8,128)} %copy.96), calls=%async_computation | async-start | bytes 1310720 | tf_op jit(solution)/shard_map/all_to_all | solution.py:121
where the time goes:
time: 78.4 us; the launch traced here: 77.9 us
  blocking collectives  37.7 us (48%)
  waiting for transfers between devices  18.3 us (23%)
  local copies, waits for them, and re-layouts  8.64 us (11%)
  starting transfers between devices  5.54 us (7%)
  other arithmetic  4.24 us (5%)
  matrix products  3.09 us (4%)
    all_gather x1, blocking collectives, per_device(): gathered = lax.all_gather(packed, 'row', axis=0, tiled=True)  32.5 us
    all_to_all x1, waiting for transfers between devices, per_device(): lax.all_to_all(outgoing, ('ctx', 'row'), split_axis=0, concat_axis=0, til...  18.3 us
    all_to_all x1, starting transfers between devices, per_device(): lax.all_to_all(outgoing, ('ctx', 'row'), split_axis=0, concat_axis=0, til...  5.54 us
    all_gather x1, blocking collectives, per_device(): whole = lax.all_gather(result, 'ctx', axis=0, tiled=True)  5.18 us
    unnamed x31, local copies, waits for them, and re-layouts  3.59 us
    dot_general x3, matrix products, block_stats(): jnp.einsum(einsum_form, weights, values, preferred_element_type=jnp.float32)  1.75 us
  transfers between devices with their start and end apart: 1, of which 1 were waited for; matrix products, arithmetic and copies ran while one was open for 1% of the time, Pallas kernels for 0%

commit v1 on v0

--- a/solution.py
+++ b/solution.py
@@ -9,6 +9,17 @@
 HD = 128
 LANES = 128
 MASKED_SCORE = -1e30
+
+
+def gather_by_hops(value, name, dim):
+    size = lax.axis_size(name)
+    right = [(i, (i + 1) % size) for i in range(size)]
+    shards = [value]
+    for far in range(1, size):
+        shards = [lax.ppermute(shards[0], name, right), *shards]
+    whole = jnp.concatenate(shards, axis=dim)
+    shift = (lax.axis_index(name) + 1) * shards[-1].shape[dim]
+    return jnp.roll(whole, shift, axis=dim)
 
 
 def block_stats(scores, valid_mask, values, einsum_form):
@@ -81,7 +92,7 @@
     query_cols = step_count * feature_width
     id_cols = jnp.broadcast_to(prefix_id.astype(jnp.bfloat16)[:, None], (rows_dev, LANES))
     packed = jnp.concatenate([queries.reshape(rows_dev, query_cols), id_cols], axis=1)
-    gathered = lax.all_gather(packed, "row", axis=0, tiled=True)
+    gathered = gather_by_hops(packed, "row", 0)
     total_rows = gathered.shape[0]
     every_query = gathered[:, :query_cols].reshape(total_rows, step_count, KVH, groups, HD)
     every_prefix = gathered[:, query_cols].astype(jnp.int32)

time: 78.4 us -> 88.3 us (1.13)
  waiting for transfers between devices: 18.3 us -> 59.1 us
  blocking collectives: 37.7 us -> 5.18 us
  local copies, waits for them, and re-layouts: 8.64 us -> 12.4 us
  other arithmetic: 4.24 us -> 3.12 us
  matrix products: 3.09 us -> 2.14 us
    ppermute x0 -> x7, waiting for transfers between devices: none -> 40.7 us  [gather_by_hops(): shards = [lax.ppermute(shards[0], name, right), *shards]]
    all_gather x1 -> x0, blocking collectives: 32.5 us -> none  [per_device(): gathered = lax.all_gather(packed, 'row', axis=0, tiled=True)]
    concatenate x0 -> x1, local copies, waits for them, and re-layouts: none -> 3.19 us  [gather_by_hops(): return jnp.roll(whole, shift, axis=dim)]
    ppermute x0 -> x7, starting transfers between devices: none -> 3.01 us  [gather_by_hops(): shards = [lax.ppermute(shards[0], name, right), *shards]]
    all_to_all x1, starting transfers between devices: 5.54 us -> 2.75 us  [per_device(): lax.all_to_all(outgoing, ('ctx', 'row'), split_axis=0, concat_axis=0, til...]
    unnamed x31 -> x22, local copies, waits for them, and re-layouts: 3.59 us -> 2.23 us
    reshape x1, local copies, waits for them, and re-layouts: 0.27 us -> 1.35 us  [per_device(): flat_keys = pool_keys.reshape(slot_count * page_len, KVH, HD)]
    dot_general x3, matrix products: 1.75 us -> 0.81 us  [block_stats(): jnp.einsum(einsum_form, weights, values, preferred_element_type=jnp.float32)]
  transfers between devices with their start and end apart: 1 -> 8, of which waited for: 1 -> 8; matrix products, arithmetic and copies ran while one was open for 1% -> 6% of each run, Pallas kernels for 0% -> 0%
where the time goes in v1:
time: 88.3 us; the launch traced here: 88 us
  waiting for transfers between devices  59.1 us (67%)
  local copies, waits for them, and re-layouts  12.4 us (14%)
  starting transfers between devices  5.75 us (7%)
  blocking collectives  5.18 us (6%)
  other arithmetic  3.12 us (4%)
  matrix products  2.14 us (2%)
    ppermute x7, waiting for transfers between devices, gather_by_hops(): shards = [lax.ppermute(shards[0], name, right), *shards]  40.7 us
    all_to_all x1, waiting for transfers between devices, per_device(): lax.all_to_all(outgoing, ('ctx', 'row'), split_axis=0, concat_axis=0, til...  18.3 us
    all_gather x1, blocking collectives, per_device(): whole = lax.all_gather(result, 'ctx', axis=0, tiled=True)  5.18 us
    concatenate x1, local copies, waits for them, and re-layouts, gather_by_hops(): return jnp.roll(whole, shift, axis=dim)  3.19 us
    ppermute x7, starting transfers between devices, gather_by_hops(): shards = [lax.ppermute(shards[0], name, right), *shards]  3.01 us
    all_to_all x1, starting transfers between devices, per_device(): lax.all_to_all(outgoing, ('ctx', 'row'), split_axis=0, concat_axis=0, til...  2.75 us
    unnamed x22, local copies, waits for them, and re-layouts  2.23 us
  transfers between devices with their start and end apart: 8, of which 8 were waited for; matrix products, arithmetic and copies ran while one was open for 6% of the time, Pallas kernels for 0%

profile of v1, /device:TPU:0, one launch (start us, length us, event | category | flops | bytes accessed | tf_op | source)
XLA Modules:
  0.0 88.0 jit_solution(12798678446265952516)
XLA Ops:
  0.0 0.7 convert_element_type.32
  0.7 0.8 copy.117
  1.6 3.0 %collective-permute-start = (bf16[2,8320]{1,0:T(2,128)(2,1)S(1)}, bf16[2,8320]{1,0:T(2,128)(2,1)S(1)}, u32[]{:S(2)}, u32[]{:S(2)}) collective-permute-start(bf16[2,8320]{1,0:T(2,128)(2,1)S(1)} %pad_maximum_fusion), channel_id=1, source_target_pairs={{0,1},{1,2},{2,3},{3,4},{4,5},{5,6},{6,7},{7,0},{8,9},{9,10},{10,1... | collective-permute-start | bytes 99848 | tf_op jit(solution)/shard_map/ppermute | solution.py:19
  4.6 4.9 %collective-permute-done = bf16[2,8320]{1,0:T(2,128)(2,1)S(1)} collective-permute-done((bf16[2,8320]{1,0:T(2,128)(2,1)S(1)}, bf16[2,8320]{1,0:T(2,128)(2,1)S(1)}, u32[]{:S(2)}, u32[]{:S(2)}) %collective-permute-start) | collective-permute-done | bytes 33312 | tf_op jit(solution)/shard_map/ppermute | solution.py:19
  9.5 0.2 fusion.16
  9.7 6.4 %collective-permute-done.1 = bf16[2,8320]{1,0:T(2,128)(2,1)S(1)} collective-permute-done((bf16[2,8320]{1,0:T(2,128)(2,1)S(1)}, bf16[2,8320]{1,0:T(2,128)(2,1)S(1)}, u32[]{:S(2)}, u32[]{:S(2)}) %collective-permute-start.1) | collective-permute-done | bytes 33312 | tf_op jit(solution)/shard_map/ppermute | solution.py:19
  16.2 6.6 %collective-permute-done.2 = bf16[2,8320]{1,0:T(2,128)(2,1)S(1)} collective-permute-done((bf16[2,8320]{1,0:T(2,128)(2,1)S(1)}, bf16[2,8320]{1,0:T(2,128)(2,1)S(1)}, u32[]{:S(2)}, u32[]{:S(2)}) %collective-permute-start.2) | collective-permute-done | bytes 33312 | tf_op jit(solution)/shard_map/ppermute | solution.py:19
  22.8 0.2 compare_reduce_fusion
  23.0 0.1 and.28
  23.2 0.1 add.87
  23.4 6.0 %collective-permute-done.3 = bf16[2,8320]{1,0:T(2,128)(2,1)S(1)} collective-permute-done((bf16[2,8320]{1,0:T(2,128)(2,1)S(1)}, bf16[2,8320]{1,0:T(2,128)(2,1)S(1)}, u32[]{:S(2)}, u32[]{:S(2)}) %collective-permute-start.3) | collective-permute-done | bytes 33312 | tf_op jit(solution)/shard_map/ppermute | solution.py:19
  29.5 1.3 %reshape.130 = bf16[1024,4,128]{2,1,0:T(4,128)(2,1)S(1)} reshape(bf16[16,64,512]{2,1,0:T(8,128)(2,1)} %param.16) | data formatting | bytes 2097152 | tf_op jit(solution)/shard_map/reshape | solution.py:76
  30.9 5.5 %collective-permute-done.4 = bf16[2,8320]{1,0:T(2,128)(2,1)S(1)} collective-permute-done((bf16[2,8320]{1,0:T(2,128)(2,1)S(1)}, bf16[2,8320]{1,0:T(2,128)(2,1)S(1)}, u32[]{:S(2)}, u32[]{:S(2)}) %collective-permute-start.4) | collective-permute-done | bytes 33312 | tf_op jit(solution)/shard_map/ppermute | solution.py:19
  36.4 0.5 select_reduce_fusion
  36.9 6.1 %collective-permute-done.5 = bf16[2,8320]{1,0:T(2,128)(2,1)S(1)} collective-permute-done((bf16[2,8320]{1,0:T(2,128)(2,1)S(1)}, bf16[2,8320]{1,0:T(2,128)(2,1)S(1)}, u32[]{:S(2)}, u32[]{:S(2)}) %collective-permute-start.5) | collective-permute-done | bytes 33312 | tf_op jit(solution)/shard_map/ppermute | solution.py:19
  43.0 0.3 convert_reduce_fusion
  43.2 1.1 %reshape.132 = bf16[1024,4,128]{2,1,0:T(4,128)(2,1)} reshape(bf16[16,64,512]{2,1,0:T(8,128)(2,1)S(1)} %copy-done.1) | data formatting | bytes 2097152 | tf_op jit(solution)/shard_map/reshape | solution.py:77
  44.4 5.2 %collective-permute-done.6 = bf16[2,8320]{1,0:T(2,128)(2,1)S(1)} collective-permute-done((bf16[2,8320]{1,0:T(2,128)(2,1)S(1)}, bf16[2,8320]{1,0:T(2,128)(2,1)S(1)}, u32[]{:S(2)}, u32[]{:S(2)}) %collective-permute-start.6) | collective-permute-done | bytes 33312 | tf_op jit(solution)/shard_map/ppermute | solution.py:19
  49.6 3.2 %concatenate.16 = bf16[32,8320]{1,0:T(8,128)(2,1)S(1)} concatenate(bf16[2,8320]{1,0:T(2,128)(2,1)S(1)} %collective-permute-done.6, bf16[2,8320]{1,0:T(2,128)(2,1)S(1)} %collective-permute-done.5, bf16[2,8320]{1,0:T(2,128)(2,1)S(1)} %collective-permute-done.4, bf16[2,8320]{1,0:T(2,128)(2,1)S(1)} %collective-permute-done.3, bf16[2,8320]{1,0:T(2,128)(2,1)S(1)} %collective-permute-done.2, ...), dimensions={0} | concatenate | bytes 1064960 | tf_op jit(solution)/shard_map/jit(_roll_dynamic)/concatenate | solution.py:22
  52.8 0.2 convert_reduce_fusion.3
  53.0 0.1 dynamic-slice_bitcast_fusion
  53.1 0.6 gather_fusion
  53.7 0.4 copy-done.3
  54.1 0.6 gather_fusion.1
  54.7 0.2 broadcast_select_fusion.1
  54.8 0.1 reshape.127
  55.0 0.1 reshape.128
  55.1 0.5 fusion.22
  55.7 0.5 convert_reduce_fusion.1
  56.1 0.3 fusion.10
  56.5 0.1 reshape.135
  56.6 0.1 reshape.134
  56.8 0.9 %copy-done.2 = bf16[1024,4,128]{2,1,0:T(4,128)(2,1)S(1)} copy-done((bf16[1024,4,128]{2,1,0:T(4,128)(2,1)S(1)}, bf16[1024,4,128]{2,1,0:T(4,128)(2,1)}, u32[]{:S(2)}) %copy-start.2) | copy-done | bytes 1048600
  57.7 0.3 fusion.4
  58.2 0.3 copy.161
  58.5 1.2 %copy.96 = f32[32,33,128]{2,1,0:T(8,128)} copy(f32[32,33,128]{2,0,1:T(8,128)S(1)} %bitcast.57) | data formatting | bytes 1081344 | tf_op jit(solution)/shard_map/reshape | solution.py:131
  59.7 2.7 %all-to-all-start = ((f32[32,33,128]{2,1,0:T(8,128)}), f32[32,33,128]{2,1,0:T(8,128)S(1)}, u32[]{:S(2)}, u32[]{:S(2)}) async-start(f32[32,33,128]{2,1,0:T(8,128)} %copy.96), calls=%async_computation | async-start | bytes 1310720 | tf_op jit(solution)/shard_map/all_to_all | solution.py:132
  62.4 0.3 select_reduce_fusion.1
  62.7 0.1 reshape.140
  62.8 0.1 convert_reduce_fusion.2
  62.9 0.2 convolution_bitcast_fusion
  63.2 0.1 reshape.143
  63.2 18.3 %all-to-all-done = f32[32,33,128]{2,1,0:T(8,128)S(1)} async-done(((f32[32,33,128]{2,1,0:T(8,128)}), f32[32,33,128]{2,1,0:T(8,128)S(1)}, u32[]{:S(2)}, u32[]{:S(2)}) %all-to-all-start) | async-done | bytes 540704 | tf_op jit(solution)/shard_map/all_to_all | solution.py:132
  81.7 0.1 fusion.17
  81.9 0.2 fusion.8
  82.1 0.1 divide_convert_fusion
  82.2 5.2 %all_gather.3 = bf16[128,128]{1,0:T(8,128)(2,1)S(1)} all-gather(bf16[32,128]{1,0:T(8,128)(2,1)S(1)} %divide_convert_fusion), channel_id=1, replica_groups=mesh['ctx'=4,'row'=8] {'ctx'}, dimensions={0}, use_global_device_ids=true | all-gather | bytes 40960 | tf_op jit(solution)/shard_map/all_gather | solution.py:148
  87.3 0.6 reshape.144
  (51 shorter events, 1.1 us)
Async XLA Ops:
  0.0 53.1 %copy-start = (bf16[8,32,512]{2,1,0:T(8,128)(2,1)S(1)}, bf16[8,32,512]{2,1,0:T(8,128)(2,1)}, u32[]{:S(2)}) copy-start(bf16[8,32,512]{2,1,0:T(8,128)(2,1)} %param.15) | copy-start | bytes 786436
  1.6 7.9 %collective-permute-start = (bf16[2,8320]{1,0:T(2,128)(2,1)S(1)}, bf16[2,8320]{1,0:T(2,128)(2,1)S(1)}, u32[]{:S(2)}, u32[]{:S(2)}) collective-permute-start(bf16[2,8320]{1,0:T(2,128)(2,1)S(1)} %pad_maximum_fusion), channel_id=1, source_target_pairs={{0,1},{1,2},{2,3},{3,4},{4,5},{5,6},{6,7},{7,0},{8,9},{9,10},{10,1... | collective-permute-start | bytes 99848 | tf_op jit(solution)/shard_map/ppermute | solution.py:19
  4.6 4.9 %copy-start.6 = (s32[2,32]{1,0:T(2,128)S(1)}, s32[2,32]{1,0:T(2,128)}, u32[]{:S(2)}) copy-start(s32[2,32]{1,0:T(2,128)} %param.18) | copy-start | bytes 772
  9.5 6.6 %collective-permute-start.1 = (bf16[2,8320]{1,0:T(2,128)(2,1)S(1)}, bf16[2,8320]{1,0:T(2,128)(2,1)S(1)}, u32[]{:S(2)}, u32[]{:S(2)}) collective-permute-start(bf16[2,8320]{1,0:T(2,128)(2,1)S(1)} %collective-permute-done), channel_id=1, source_target_pairs={{0,1},{1,2},{2,3},{3,4},{4,5},{5,6},{6,7},{7,0},{8,9},{9,10},{10,1... | collective-permute-start | bytes 99848 | tf_op jit(solution)/shard_map/ppermute | solution.py:19
  16.2 6.6 %collective-permute-start.2 = (bf16[2,8320]{1,0:T(2,128)(2,1)S(1)}, bf16[2,8320]{1,0:T(2,128)(2,1)S(1)}, u32[]{:S(2)}, u32[]{:S(2)}) collective-permute-start(bf16[2,8320]{1,0:T(2,128)(2,1)S(1)} %collective-permute-done.1), channel_id=1, source_target_pairs={{0,1},{1,2},{2,3},{3,4},{4,5},{5,6},{6,7},{7,0},{8,9},{9,10},{10,1... | collective-permute-start | bytes 99848 | tf_op jit(solution)/shard_map/ppermute | solution.py:19
  22.8 6.6 %collective-permute-start.3 = (bf16[2,8320]{1,0:T(2,128)(2,1)S(1)}, bf16[2,8320]{1,0:T(2,128)(2,1)S(1)}, u32[]{:S(2)}, u32[]{:S(2)}) collective-permute-start(bf16[2,8320]{1,0:T(2,128)(2,1)S(1)} %collective-permute-done.2), channel_id=1, source_target_pairs={{0,1},{1,2},{2,3},{3,4},{4,5},{5,6},{6,7},{7,0},{8,9},{9,10},{10,1... | collective-permute-start | bytes 99848 | tf_op jit(solution)/shard_map/ppermute | solution.py:19
  23.2 6.3 %copy-start.4 = (bf16[2,2,4096]{2,1,0:T(2,128)(2,1)S(1)}, bf16[2,2,4096]{2,1,0:T(2,128)(2,1)}, u32[]{:S(2)}) copy-start(bf16[2,2,4096]{2,1,0:T(2,128)(2,1)} %param.12) | copy-start | bytes 98308
  23.3 6.1 %copy-start.7 = (s32[2]{0:T(128)S(1)}, s32[2]{0:T(128)}, u32[]{:S(2)}) copy-start(s32[2]{0:T(128)} %param.19) | copy-start | bytes 28
  29.4 7.0 %collective-permute-start.4 = (bf16[2,8320]{1,0:T(2,128)(2,1)S(1)}, bf16[2,8320]{1,0:T(2,128)(2,1)S(1)}, u32[]{:S(2)}, u32[]{:S(2)}) collective-permute-start(bf16[2,8320]{1,0:T(2,128)(2,1)S(1)} %collective-permute-done.3), channel_id=1, source_target_pairs={{0,1},{1,2},{2,3},{3,4},{4,5},{5,6},{6,7},{7,0},{8,9},{9,10},{10,1... | collective-permute-start | bytes 99848 | tf_op jit(solution)/shard_map/ppermute | solution.py:19
  36.3 6.6 %collective-permute-start.5 = (bf16[2,8320]{1,0:T(2,128)(2,1)S(1)}, bf16[2,8320]{1,0:T(2,128)(2,1)S(1)}, u32[]{:S(2)}, u32[]{:S(2)}) collective-permute-start(bf16[2,8320]{1,0:T(2,128)(2,1)S(1)} %collective-permute-done.4), channel_id=1, source_target_pairs={{0,1},{1,2},{2,3},{3,4},{4,5},{5,6},{6,7},{7,0},{8,9},{9,10},{10,1... | collective-permute-start | bytes 99848 | tf_op jit(solution)/shard_map/ppermute | solution.py:19
  36.4 6.9 %copy-start.1 = (bf16[16,64,512]{2,1,0:T(8,128)(2,1)S(1)}, bf16[16,64,512]{2,1,0:T(8,128)(2,1)}, u32[]{:S(2)}) copy-start(bf16[16,64,512]{2,1,0:T(8,128)(2,1)} %param.17) | copy-start | bytes 3145732
  43.0 6.6 %collective-permute-start.6 = (bf16[2,8320]{1,0:T(2,128)(2,1)S(1)}, bf16[2,8320]{1,0:T(2,128)(2,1)S(1)}, u32[]{:S(2)}, u32[]{:S(2)}) collective-permute-start(bf16[2,8320]{1,0:T(2,128)(2,1)S(1)} %collective-permute-done.5), channel_id=1, source_target_pairs={{0,1},{1,2},{2,3},{3,4},{4,5},{5,6},{6,7},{7,0},{8,9},{9,10},{10,1... | collective-permute-start | bytes 99848 | tf_op jit(solution)/shard_map/ppermute | solution.py:19
  53.1 1.0 %copy-start.3 = (bf16[8,32,512]{2,1,0:T(8,128)(2,1)S(1)}, bf16[8,32,512]{2,1,0:T(8,128)(2,1)}, u32[]{:S(2)}) copy-start(bf16[8,32,512]{2,1,0:T(8,128)(2,1)} %param.14) | copy-start | bytes 786436
  56.4 1.2 %copy-start.2 = (bf16[1024,4,128]{2,1,0:T(4,128)(2,1)S(1)}, bf16[1024,4,128]{2,1,0:T(4,128)(2,1)}, u32[]{:S(2)}) copy-start(bf16[1024,4,128]{2,1,0:T(4,128)(2,1)} %reshape.132) | copy-start | bytes 3145732
  59.7 2.8 %copy-start.8 = (bf16[2,2,512]{2,1,0:T(2,128)(2,1)S(1)}, bf16[2,2,512]{2,1,0:T(2,128)(2,1)}, u32[]{:S(2)}) copy-start(bf16[2,2,512]{2,1,0:T(2,128)(2,1)} %param.20) | copy-start | bytes 12292
  59.7 3.3 %copy-start.5 = (bf16[2,2,512]{2,1,0:T(2,128)(2,1)S(1)}, bf16[2,2,512]{2,1,0:T(2,128)(2,1)}, u32[]{:S(2)}) copy-start(bf16[2,2,512]{2,1,0:T(2,128)(2,1)} %param.21) | copy-start | bytes 12292
  59.7 21.9 %all-to-all-start = ((f32[32,33,128]{2,1,0:T(8,128)}), f32[32,33,128]{2,1,0:T(8,128)S(1)}, u32[]{:S(2)}, u32[]{:S(2)}) async-start(f32[32,33,128]{2,1,0:T(8,128)} %copy.96), calls=%async_computation | async-start | bytes 1310720 | tf_op jit(solution)/shard_map/all_to_all | solution.py:132
